TPU v7x, 512 devices: a whole 4x4x16 slice. The times are simulated.
512 devices in a mesh: seq: 64 (over x, z), tp: 8 (over y, core).
Axes of the slice: x: 4, y: 4, z: 16, core: 2. Of those that a mesh axis runs over, the one named last changes fastest.
Arguments:
- queries: bfloat16 [64, 4, 8192], P('seq', None, 'tp'), may hold values from -40 to 40
- new_keys: bfloat16 [64, 4, 1024], P('seq', None, 'tp'), may hold values from -6 to 6
- new_values: bfloat16 [64, 4, 1024], P('seq', None, 'tp'), may hold values from -6 to 6
- prefix_keys: bfloat16 [8, 12288, 1024], P(None, 'seq', 'tp'), may hold values from -8 to 8
- prefix_values: bfloat16 [8, 12288, 1024], P(None, 'seq', 'tp'), may hold values from -6 to 6
- page_keys: bfloat16 [1024, 64, 1024], P('seq', None, 'tp'), may hold values from -6 to 6
- page_values: bfloat16 [1024, 64, 1024], P('seq', None, 'tp'), may hold values from -6 to 6
- out_weight: bfloat16 [8192, 8192], P('tp', 'seq'), may hold values from -0.5 to 0.5
- group_of: int32 [64], replicated, may hold values from 0 to 7, as said below
- prefix_len: int32 [8], replicated, may hold values from 2 to 12288, as said below
- total_len: int32 [64], replicated, may hold values from 3 to 16384, as said below
- page_owner: int32 [1024], P('seq'), may hold values from 0 to 63, as said below
- page_slot: int32 [1024], P('seq'), may hold values from 0 to 63, as said below
- new_valid: int32 [64, 4], replicated, may hold values from 0 to 1, as said below
Outputs:
- attn_out: bfloat16 [256, 8192], P('tp', 'seq')
Inputs may be any that keep to these rules, and one draw needn't show every extreme that they name: `group_of`: every one of the 8 groups has at least one request. `prefix_len`: some group's prefix holds exactly 12288 tokens. `page_owner`: every request owns at least one page and at most 64 pages; one request owns exactly 64. `page_slot`: the pages of one request carry the slots 0, 1, 2 and so on, each once. A request's pages are full except the one of its highest slot, which holds 1 to 64 tokens; total_len is its group's prefix length plus these tokens. `new_valid`: each row is a run of ones followed by zeros, and its first entry is one.
All inputs are finite; a program needn't handle non-finite values.
Results may differ from a plain program's by a relative error of at most 0.022.
Values may be sent and summed in bfloat16 or wider, within the bound.
No kernel may reach another device: no remote copies, remote signals or barrier semaphores. Data moves between devices by JAX's collectives and lax.ppermute only.
A program may use at most 192 MiB of HBM per device.

v0:
```python
import jax
import jax.numpy as jnp
from jax import lax
from jax.sharding import PartitionSpec as P

HEAD_DIM = 128
HPK = 8
GROUPS = 8
NEW = 4
NEG = -1e30


def local(
    queries,
    new_keys,
    new_values,
    prefix_keys,
    prefix_values,
    page_keys,
    page_values,
    out_weight,
    group_of,
    prefix_len,
    total_len,
    page_owner,
    page_slot,
    new_valid,
):
    req_dev = queries.shape[0]
    seq_count = lax.axis_size("seq")
    requests = req_dev * seq_count
    kv_local = new_keys.shape[2] // HEAD_DIM
    heads_local = kv_local * HPK
    score_scale = HEAD_DIM ** (-0.5)
    seq_idx = lax.axis_index("seq")
    gathered = lax.all_gather(queries, "seq", axis=0, tiled=True)
    query_all = gathered.reshape(requests, NEW, kv_local, HPK, HEAD_DIM)
    group_hot = group_of[:, None] == jnp.arange(GROUPS, dtype=jnp.int32)[None, :]
    own_prefix = jnp.sum(jnp.where(group_hot, prefix_len[None, :], 0), axis=1)
    suffix_len = total_len - own_prefix
    pre_dev = prefix_keys.shape[1]
    page_count = page_keys.shape[0]
    page_len = page_keys.shape[1]
    keys = jnp.concatenate(
        [
            prefix_keys.reshape(GROUPS * pre_dev, kv_local, HEAD_DIM),
            page_keys.reshape(page_count * page_len, kv_local, HEAD_DIM),
            new_keys.reshape(req_dev * NEW, kv_local, HEAD_DIM),
        ],
        axis=0,
    )
    values = jnp.concatenate(
        [
            prefix_values.reshape(GROUPS * pre_dev, kv_local, HEAD_DIM),
            page_values.reshape(page_count * page_len, kv_local, HEAD_DIM),
            new_values.reshape(req_dev * NEW, kv_local, HEAD_DIM),
        ],
        axis=0,
    )
    req_ids = jnp.arange(requests, dtype=jnp.int32)
    positions = seq_idx * pre_dev + jnp.arange(pre_dev, dtype=jnp.int32)
    pre_live = positions[None, :] < prefix_len[:, None]
    pre_mask = group_hot[:, :, None] & pre_live[None, :, :]
    pre_mask = pre_mask.reshape(requests, 1, GROUPS * pre_dev)
    pre_mask = jnp.broadcast_to(pre_mask, (requests, NEW, GROUPS * pre_dev))
    owner_hot = req_ids[:, None] == page_owner[None, :]
    offsets = page_slot[:, None] * page_len + jnp.arange(page_len, dtype=jnp.int32)[None, :]
    page_live = offsets[None, :, :] < suffix_len[:, None, None]
    page_mask = (owner_hot[:, :, None] & page_live).reshape(requests, 1, page_count * page_len)
    page_mask = jnp.broadcast_to(page_mask, (requests, NEW, page_count * page_len))
    new_owner = seq_idx * req_dev + jnp.arange(req_dev, dtype=jnp.int32)
    tok = jnp.arange(NEW, dtype=jnp.int32)
    causal = tok[None, :] <= tok[:, None]
    new_live = new_valid == 1
    new_mask = (
        (req_ids[:, None, None, None] == new_owner[None, None, :, None])
        & causal[None, :, None, :]
        & new_live[:, None, None, :]
    ).reshape(requests, NEW, req_dev * NEW)
    key_mask = jnp.concatenate([pre_mask, page_mask, new_mask], axis=2)
    key_mask = key_mask[:, :, None, None, :]
    scores = (
        jnp.einsum("rjkhd,nkd->rjkhn", query_all, keys, preferred_element_type=jnp.float32)
        * score_scale
    )
    masked = jnp.where(key_mask, scores, NEG)
    row_peak = jnp.max(masked, axis=-1)
    weights = jnp.where(key_mask, jnp.exp(masked - row_peak[..., None]), 0.0)
    row_total = jnp.sum(weights, axis=-1)
    out = jnp.einsum(
        "rjkhn,nkd->rjkhd", weights.astype(jnp.bfloat16), values, preferred_element_type=jnp.float32
    )
    top_peak = lax.pmax(row_peak, "seq")
    factor = jnp.exp(row_peak - top_peak)
    final_total, final_out = lax.psum((row_total * factor, out * factor[..., None]), "seq")
    valid_rows = new_valid.astype(jnp.float32)[:, :, None, None, None]
    attention = (final_out / final_total[..., None] * valid_rows).astype(jnp.bfloat16)
    attention = attention.reshape(requests * NEW, heads_local * HEAD_DIM)
    terms = jnp.dot(attention, out_weight, preferred_element_type=jnp.float32)
    summed = lax.psum_scatter(terms.astype(jnp.bfloat16), "tp", scatter_dimension=0, tiled=True)
    return summed


def solution(mesh):
    placed = (
        P("seq", None, "tp"),
        P("seq", None, "tp"),
        P("seq", None, "tp"),
        P(None, "seq", "tp"),
        P(None, "seq", "tp"),
        P("seq", None, "tp"),
        P("seq", None, "tp"),
        P("tp", "seq"),
        P(),
        P(),
        P(),
        P("seq"),
        P("seq"),
        P(),
    )
    return jax.shard_map(
        local, mesh=mesh, in_specs=placed, out_specs=P("tp", "seq"), check_vma=False
    )
```

profile of v0, /device:TPU:4, one launch (start us, length us, event | category | flops | bytes accessed | tf_op | source)
XLA Modules:
  0.0 738.8 jit_solution(732492033588366109)
XLA Ops:
  6.5 0.0 copy-start
  6.5 0.0 all-reduce.2.cloned.1.call-start
  6.5 0.8 broadcast_reduce_fusion.1
  7.3 0.7 iota_compare_fusion.1
  8.1 0.8 select_reduce_fusion
  9.0 0.1 lt.39
  9.0 0.1 lt.41
  9.1 0.1 and.61
  9.3 0.3 and.62
  9.5 0.7 broadcast_compare_fusion
  10.2 0.1 copy.20
  10.3 0.7 iota_compare_fusion
  11.0 0.2 and.65
  11.2 0.2 and.66
  11.4 0.7 broadcast_multiply_fusion
  12.1 0.1 broadcast_reduce_fusion
  12.2 0.1 add.40
  12.2 0.1 add.42
  12.3 106.2 %all_gather.3 = bf16[64,4,1024]{2,1,0:T(4,128)(2,1)S(1)} all-gather(bf16[1,4,1024]{2,1,0:T(4,128)(2,1)} %param.14), channel_id=1, replica_groups=mesh['seq'=64,'tp'=8] {'seq'}, dimensions={0}, use_global_device_ids=true | all-gather | bytes 532480 | tf_op jit(solution)/shard_map/all_gather | solution.py:36
  118.6 0.2 reshape.221
  118.8 0.1 broadcast_and_fusion
  118.9 0.7 sub.14
  119.5 0.1 and_and_fusion
  119.6 0.1 compare_and_fusion
  119.7 0.1 broadcast_in_dim.30
  119.8 0.1 broadcast_in_dim.33
  119.9 0.1 pad_add_fusion
  120.0 0.0 copy-start.3
  120.0 0.0 copy-start.4
  120.0 0.0 copy-start.5
  120.0 5.5 fusion
  125.5 0.0 copy-start.1
  125.5 7.3 copy-done.1
  132.8 7.2 fusion.1
  140.0 236.7 %pmax.7 = f32[64,4,1,8]{0,3,1,2:T(8,128)S(1)} all-reduce(f32[64,4,1,8]{0,3,1,2:T(8,128)S(1)} %bitcast.79), channel_id=1, replica_groups=mesh['seq'=64,'tp'=8] {'seq'}, use_global_device_ids=true, to_apply=%region_2.3 | all-reduce | flops 2048 | bytes 16384 | tf_op jit(solution)/shard_map/pmax | solution.py:93
  376.8 0.0 copy-done.3
  376.8 0.0 copy-done.4
  376.8 0.0 copy-done.5
  376.8 0.0 copy-start.2
  376.8 10.4 %fusion.13 = f32[64,4,1,8,128]{4,0,3,1,2:T(8,128)} fusion(f32[2564,64,4,8]{0,1,3,2:T(8,128)} %copy-done.1, f32[64,4,8]{0,2,1:T(8,128)S(1)} %get-tuple-element.7, pred[64,4,2564]{2,0,1:T(8,128)(4,1)S(1)} %pad_add_fusion, bf16[4,1,128]{2,0,1:T(4,128)(2,1)S(1)} %bitcast.85, bf16[1024,1,128]{2,0,1:T(8,128)(2,1)S(1)} %bitcast.83, ...), kind=kOutput, calls=%fused_computation.11 | convolution fusion | flops 1372761088 | bytes 23382016 | tf_op jit(solution)/shard_map/rjkhn,nkd->rjkhd/dot_general | solution.py:90
  387.2 0.0 all-reduce.2.cloned.1.call-update
  387.2 0.0 reduce-scatter.2.cloned.1.call-start
  387.3 0.0 copy-done.2
  387.3 266.2 %psum.15 = f32[64,4,8]{0,2,1:T(8,128)S(1)} all-reduce(f32[64,4,8]{0,2,1:T(8,128)S(1)} %get-tuple-element.5), channel_id=1, replica_groups=mesh['seq'=64,'tp'=8] {'seq'}, use_global_device_ids=true, to_apply=%region_5.6 | all-reduce | flops 2048 | bytes 16384 | tf_op jit(solution)/shard_map/psum | solution.py:95
  653.5 37.7 %all-reduce.2.cloned.1.call-done = f32[64,4,1,8,128]{4,0,3,1,2:T(8,128)} async-done(((f32[64,4,1,8,128]{4,0,3,1,2:T(8,128)}), f32[64,4,1,8,128]{4,0,3,1,2:T(8,128)}) %all-reduce.2.cloned.1.call-update) | async-done | bytes 1048592 | tf_op jit(solution)/shard_map/psum | solution.py:95
  691.2 1.6 multiply_convert_fusion
  692.8 0.3 copy.23
  693.1 0.0 copy-done
  693.2 0.9 convolution_convert_fusion
  694.1 0.0 reduce-scatter.2.cloned.1.call-update
  694.1 37.9 %reduce-scatter.2.cloned.1.call-done = bf16[32,128]{1,0:T(8,128)(2,1)} async-done(((bf16[256,128]{1,0:T(8,128)(2,1)}), bf16[32,128]{1,0:T(8,128)(2,1)}) %reduce-scatter.2.cloned.1.call-update) | async-done | bytes 8208 | tf_op jit(solution)/shard_map/reduce_scatter | solution.py:100
  (9 shorter events, 0.0 us)
Async XLA Ops:
  6.5 686.6 %copy-start = (bf16[1024,128]{1,0:T(8,128)(2,1)S(1)}, bf16[1024,128]{1,0:T(8,128)(2,1)}, u32[]{:S(2)}) copy-start(bf16[1024,128]{1,0:T(8,128)(2,1)} %param.21) | copy-start | bytes 786436
  6.5 684.6 %all-reduce.2.cloned.1.call-start = ((), (), s32[]{:S(2)}) async-start(), calls=%async_computation.1 | async-start | bytes 2097152 | tf_op jit(solution)/shard_map/psum | solution.py:95
  120.0 256.8 %copy-start.3 = (bf16[8,192,128]{2,1,0:T(8,128)(2,1)S(1)}, bf16[8,192,128]{2,1,0:T(8,128)(2,1)}, u32[]{:S(2)}) copy-start(bf16[8,192,128]{2,1,0:T(8,128)(2,1)} %param.18) | copy-start | bytes 1179652
  120.0 256.8 %copy-start.4 = (bf16[16,64,128]{2,1,0:T(8,128)(2,1)S(1)}, bf16[16,64,128]{2,1,0:T(8,128)(2,1)}, u32[]{:S(2)}) copy-start(bf16[16,64,128]{2,1,0:T(8,128)(2,1)} %param.20) | copy-start | bytes 786436
  120.0 256.8 %copy-start.5 = (bf16[1,4,128]{2,1,0:T(4,128)(2,1)S(1)}, bf16[1,4,128]{2,1,0:T(4,128)(2,1)}, u32[]{:S(2)}) copy-start(bf16[1,4,128]{2,1,0:T(4,128)(2,1)} %param.16) | copy-start | bytes 3076
  125.5 7.3 copy-start.1
  376.8 10.5 %copy-start.2 = (s32[64,4]{0,1:T(4,128)S(1)}, s32[64,4]{0,1:T(4,128)}, u32[]{:S(2)}) copy-start(s32[64,4]{0,1:T(4,128)} %param.27) | copy-start | bytes 3076
  387.2 344.8 %reduce-scatter.2.cloned.1.call-start = ((), (), s32[]{:S(2)}) async-start(), calls=%async_computation.2 | async-start | bytes 73728 | tf_op jit(solution)/shard_map/reduce_scatter | solution.py:100
Sparse Core Ops, SparseCore 0:
  387.3 303.7 all-reduce.1
  694.2 37.7 reduce-scatter.1
where the time goes:
time: 739 us
  blocking collectives  609 us (82%)
  waiting for transfers between devices  75.6 us (10%)
  matrix products  16.7 us (2%)
  between operations  13.7 us (2%)
  other arithmetic  13.4 us (2%)
  local copies, waits for them, and re-layouts  10.2 us (1%)
    psum x1, blocking collectives, local(): lax.psum((row_total * factor, out * factor[..., None]), 'seq')  266 us
    pmax x1, blocking collectives, local(): top_peak = lax.pmax(row_peak, 'seq')  237 us
    all_gather x1, blocking collectives, local(): gathered = lax.all_gather(queries, 'seq', axis=0, tiled=True)  106 us
    reduce_scatter x1, waiting for transfers between devices, local(): lax.psum_scatter(terms.astype(jnp.bfloat16), 'tp', scatter_dimension=0, t...  37.9 us
    psum x1, waiting for transfers between devices, local(): lax.psum((row_total * factor, out * factor[..., None]), 'seq')  37.7 us
  transfers between devices with their start and end apart: 2, of which 2 were waited for; matrix products, arithmetic and copies ran while one was open for 0% of the time, Pallas kernels for 0%

commit v1 on v0

--- a/solution.py
+++ b/solution.py
@@ -33,7 +33,10 @@
     heads_local = kv_local * HPK
     score_scale = HEAD_DIM ** (-0.5)
     seq_idx = lax.axis_index("seq")
-    gathered = lax.all_gather(queries, "seq", axis=0, tiled=True)
+    size = lax.axis_size("seq")
+    shards = jnp.stack([queries for _ in range(size)])
+    shards = lax.all_to_all(shards, "seq", split_axis=0, concat_axis=0)
+    gathered = jnp.concatenate(shards, axis=0)
     query_all = gathered.reshape(requests, NEW, kv_local, HPK, HEAD_DIM)
     group_hot = group_of[:, None] == jnp.arange(GROUPS, dtype=jnp.int32)[None, :]
     own_prefix = jnp.sum(jnp.where(group_hot, prefix_len[None, :], 0), axis=1)

time: 739 us -> 676 us (0.915)
  the two profiles are of different devices: /device:TPU:4 before, /device:TPU:2 now
where the time goes in v1:
time: 676 us
  blocking collectives  525 us (78%)
  waiting for transfers between devices  76 us (11%)
  starting transfers between devices  18.7 us (3%)
  matrix products  16.7 us (2%)
  between operations  13.7 us (2%)
  other arithmetic  13.4 us (2%)
  local copies, waits for them, and re-layouts  11.8 us (2%)
    psum x1, blocking collectives, local(): lax.psum((row_total * factor, out * factor[..., None]), 'seq')  274 us
    pmax x1, blocking collectives, local(): top_peak = lax.pmax(row_peak, 'seq')  251 us
    reduce_scatter x1, waiting for transfers between devices, local(): lax.psum_scatter(terms.astype(jnp.bfloat16), 'tp', scatter_dimension=0, t...  37.5 us
    all_to_all x1, waiting for transfers between devices, local(): shards = lax.all_to_all(shards, 'seq', split_axis=0, concat_axis=0)  24.7 us
    all_to_all x1, starting transfers between devices, local(): shards = lax.all_to_all(shards, 'seq', split_axis=0, concat_axis=0)  18.6 us
    psum x1, waiting for transfers between devices, local(): lax.psum((row_total * factor, out * factor[..., None]), 'seq')  13.8 us
  transfers between devices with their start and end apart: 3, of which 3 were waited for; matrix products, arithmetic and copies ran while one was open for 1% of the time, Pallas kernels for 0%

profile of v1, /device:TPU:2, one launch (start us, length us, event | category | flops | bytes accessed | tf_op | source)
XLA Modules:
  0.0 675.7 jit_solution(12783928072095828557)
XLA Ops:
  6.5 0.0 copy-start
  6.5 1.7 stack.2
  8.2 18.6 %all-to-all-start = ((bf16[64,1,4,1024]{3,2,1,0:T(4,128)(2,1)}), bf16[64,1,4,1024]{3,2,1,0:T(4,128)(2,1)S(1)}, u32[]{:S(2)}, u32[]{:S(2)}) async-start(bf16[64,1,4,1024]{3,2,1,0:T(4,128)(2,1)} %stack.2), calls=%async_computation | async-start | bytes 1048576 | tf_op jit(solution)/shard_map/all_to_all | solution.py:38
  26.9 0.0 all-reduce.2.cloned.1.call-start
  26.9 0.1 lt.39
  27.0 0.7 broadcast_reduce_fusion.1
  27.8 0.1 lt.41
  27.8 0.7 iota_compare_fusion.1
  28.6 0.1 and.61
  28.7 0.3 and.62
  29.0 0.7 broadcast_compare_fusion
  29.7 0.1 copy.19
  29.8 0.7 iota_compare_fusion
  30.4 0.2 and.65
  30.6 0.2 and.66
  30.9 0.7 broadcast_multiply_fusion
  31.5 0.1 broadcast_reduce_fusion
  31.6 0.1 add.40
  31.7 0.1 add.42
  31.8 0.8 select_reduce_fusion
  32.6 0.7 sub.14
  33.3 0.1 and_and_fusion
  33.4 0.1 compare_and_fusion
  33.5 0.1 broadcast_and_fusion
  33.6 0.1 broadcast_in_dim.30
  33.7 0.1 broadcast_in_dim.33
  33.8 0.1 pad_add_fusion
  33.9 24.7 %all-to-all-done = bf16[64,1,4,1024]{3,2,1,0:T(4,128)(2,1)S(1)} async-done(((bf16[64,1,4,1024]{3,2,1,0:T(4,128)(2,1)}), bf16[64,1,4,1024]{3,2,1,0:T(4,128)(2,1)S(1)}, u32[]{:S(2)}, u32[]{:S(2)}) %all-to-all-start) | async-done | bytes 524320 | tf_op jit(solution)/shard_map/all_to_all | solution.py:38
  58.5 0.2 reshape.223
  58.7 0.0 copy-start.3
  58.7 0.0 copy-start.4
  58.8 0.0 copy-start.5
  58.8 5.5 fusion
  64.2 0.0 copy-start.1
  64.3 7.3 %copy-done.1 = f32[2564,64,4,8]{0,1,3,2:T(8,128)} copy-done((f32[2564,64,4,8]{0,1,3,2:T(8,128)}, f32[2564,64,4,8]{0,1,3,2:T(8,128)S(1)}, u32[]{:S(2)}) %copy-start.1) | copy-done | bytes 21004312
  71.6 7.2 %fusion.1 = f32[64,4,8]{0,2,1:T(8,128)S(1)} fusion(f32[2564,64,4,8]{0,1,3,2:T(8,128)S(1)} %get-tuple-element.8, f32[64,4,8]{0,2,1:T(8,128)S(1)} %get-tuple-element.7, pred[64,4,2564]{2,0,1:T(8,128)(4,1)S(1)} %pad_add_fusion), kind=kLoop, calls=%fused_computation.3 | loop fusion | flops 26253312 | bytes 21677056 | tf_op jit(solution)/shard_map/reduce_sum | solution.py:92
  78.8 251.1 %pmax.7 = f32[64,4,1,8]{0,3,1,2:T(8,128)S(1)} all-reduce(f32[64,4,1,8]{0,3,1,2:T(8,128)S(1)} %bitcast.80), channel_id=1, replica_groups=mesh['seq'=64,'tp'=8] {'seq'}, use_global_device_ids=true, to_apply=%region_2.3 | all-reduce | flops 2048 | bytes 16384 | tf_op jit(solution)/shard_map/pmax | solution.py:96
  329.9 0.0 copy-done.3
  329.9 0.0 copy-done.4
  329.9 0.0 copy-done.5
  330.0 0.0 copy-start.2
  330.0 10.4 %fusion.13 = f32[64,4,1,8,128]{4,0,3,1,2:T(8,128)} fusion(f32[2564,64,4,8]{0,1,3,2:T(8,128)} %copy-done.1, f32[64,4,8]{0,2,1:T(8,128)S(1)} %get-tuple-element.7, pred[64,4,2564]{2,0,1:T(8,128)(4,1)S(1)} %pad_add_fusion, bf16[4,1,128]{2,0,1:T(4,128)(2,1)S(1)} %bitcast.87, bf16[1024,1,128]{2,0,1:T(8,128)(2,1)S(1)} %bitcast.85, ...), kind=kOutput, calls=%fused_computation.11 | convolution fusion | flops 1372761088 | bytes 23382016 | tf_op jit(solution)/shard_map/rjkhn,nkd->rjkhd/dot_general | solution.py:93
  340.3 0.0 all-reduce.2.cloned.1.call-update
  340.4 0.0 reduce-scatter.2.cloned.1.call-start
  340.4 0.0 copy-done.2
  340.4 274.2 %psum.15 = f32[64,4,8]{0,2,1:T(8,128)S(1)} all-reduce(f32[64,4,8]{0,2,1:T(8,128)S(1)} %get-tuple-element.5), channel_id=1, replica_groups=mesh['seq'=64,'tp'=8] {'seq'}, use_global_device_ids=true, to_apply=%region_5.6 | all-reduce | flops 2048 | bytes 16384 | tf_op jit(solution)/shard_map/psum | solution.py:98
  614.6 13.8 %all-reduce.2.cloned.1.call-done = f32[64,4,1,8,128]{4,0,3,1,2:T(8,128)} async-done(((f32[64,4,1,8,128]{4,0,3,1,2:T(8,128)}), f32[64,4,1,8,128]{4,0,3,1,2:T(8,128)}) %all-reduce.2.cloned.1.call-update) | async-done | bytes 1048592 | tf_op jit(solution)/shard_map/psum | solution.py:98
  628.4 1.6 multiply_convert_fusion
  630.1 0.3 copy.22
  630.4 0.0 copy-done
  630.4 0.9 convolution_convert_fusion
  631.3 0.0 reduce-scatter.2.cloned.1.call-update
  631.4 37.5 %reduce-scatter.2.cloned.1.call-done = bf16[32,128]{1,0:T(8,128)(2,1)} async-done(((bf16[256,128]{1,0:T(8,128)(2,1)}), bf16[32,128]{1,0:T(8,128)(2,1)}) %reduce-scatter.2.cloned.1.call-update) | async-done | bytes 8208 | tf_op jit(solution)/shard_map/reduce_scatter | solution.py:103
  (9 shorter events, 0.0 us)
Async XLA Ops:
  6.5 623.9 %copy-start = (bf16[1024,128]{1,0:T(8,128)(2,1)S(1)}, bf16[1024,128]{1,0:T(8,128)(2,1)}, u32[]{:S(2)}) copy-start(bf16[1024,128]{1,0:T(8,128)(2,1)} %param.21) | copy-start | bytes 786436
  8.2 50.3 %all-to-all-start = ((bf16[64,1,4,1024]{3,2,1,0:T(4,128)(2,1)}), bf16[64,1,4,1024]{3,2,1,0:T(4,128)(2,1)S(1)}, u32[]{:S(2)}, u32[]{:S(2)}) async-start(bf16[64,1,4,1024]{3,2,1,0:T(4,128)(2,1)} %stack.2), calls=%async_computation | async-start | bytes 1048576 | tf_op jit(solution)/shard_map/all_to_all | solution.py:38
  26.9 601.6 %all-reduce.2.cloned.1.call-start = ((), (), s32[]{:S(2)}) async-start(), calls=%async_computation.2 | async-start | bytes 2097152 | tf_op jit(solution)/shard_map/psum | solution.py:98
  58.7 271.2 %copy-start.3 = (bf16[8,192,128]{2,1,0:T(8,128)(2,1)S(1)}, bf16[8,192,128]{2,1,0:T(8,128)(2,1)}, u32[]{:S(2)}) copy-start(bf16[8,192,128]{2,1,0:T(8,128)(2,1)} %param.18) | copy-start | bytes 1179652
  58.7 271.2 %copy-start.4 = (bf16[16,64,128]{2,1,0:T(8,128)(2,1)S(1)}, bf16[16,64,128]{2,1,0:T(8,128)(2,1)}, u32[]{:S(2)}) copy-start(bf16[16,64,128]{2,1,0:T(8,128)(2,1)} %param.20) | copy-start | bytes 786436
  58.8 271.2 %copy-start.5 = (bf16[1,4,128]{2,1,0:T(4,128)(2,1)S(1)}, bf16[1,4,128]{2,1,0:T(4,128)(2,1)}, u32[]{:S(2)}) copy-start(bf16[1,4,128]{2,1,0:T(4,128)(2,1)} %param.16) | copy-start | bytes 3076
  64.2 7.3 %copy-start.1 = (f32[2564,64,4,8]{0,1,3,2:T(8,128)}, f32[2564,64,4,8]{0,1,3,2:T(8,128)S(1)}, u32[]{:S(2)}) copy-start(f32[2564,64,4,8]{0,1,3,2:T(8,128)S(1)} %get-tuple-element.8) | copy-start | bytes 63012868
  330.0 10.5 %copy-start.2 = (s32[64,4]{0,1:T(4,128)S(1)}, s32[64,4]{0,1:T(4,128)}, u32[]{:S(2)}) copy-start(s32[64,4]{0,1:T(4,128)} %param.27) | copy-start | bytes 3076
  340.4 328.5 %reduce-scatter.2.cloned.1.call-start = ((), (), s32[]{:S(2)}) async-start(), calls=%async_computation.3 | async-start | bytes 73728 | tf_op jit(solution)/shard_map/reduce_scatter | solution.py:103
Sparse Core Ops, SparseCore 0:
  340.5 287.9 all-reduce.1
  631.5 37.3 reduce-scatter.1
